TPU v7x, 256 devices: a whole 4x4x8 slice. The times are simulated.
256 devices in a mesh: kv: 8 (over y, core), blk: 32 (over x, z).
Axes of the slice: x: 4, y: 4, z: 8, core: 2. Of those that a mesh axis runs over, the one named last changes fastest.
Arguments:
- queries: bfloat16 [256, 8192], P('blk', 'kv'), may hold values from -40 to 40
- draft_token_keys: bfloat16 [256, 1024], P('blk', 'kv'), may hold values from -15 to 15
- draft_token_values: bfloat16 [256, 1024], P('blk', 'kv'), may hold values from -6 to 6
- cached_key_vectors: bfloat16 [4, 4096, 1024], P(None, 'blk', 'kv'), may hold values from -40 to 40
- cached_value_vectors: bfloat16 [4, 4096, 1024], P(None, 'blk', 'kv'), may hold values from -6 to 6
- out_weight: bfloat16 [8192, 8192], P('kv', 'blk'), may hold values from -0.5 to 0.5
- lengths: int32 [4], replicated, may hold values from 256 to 4088, as said below
- parents: int32 [4, 64], replicated, may hold values from 0 to 62, as said below
- accepted_nodes: int32 [4, 8], replicated, may hold values from 0 to 62, as said below
- accepted_count: int32 [4], replicated, may hold values from 1 to 8, as said below
Outputs:
- projected: bfloat16 [256, 8192], P('kv', 'blk')
- new_cache_keys: bfloat16 [4, 4096, 1024], P(None, 'blk', 'kv')
- new_cache_values: bfloat16 [4, 4096, 1024], P(None, 'blk', 'kv')
Inputs may be any that keep to these rules, and one draw needn't show every extreme that they name: `lengths`: some request has exactly 4088, some exactly 256. parents[r, 0] = 0 and parents[r, i] < i for i >= 1. accepted_nodes[r, 0] = 0 and accepted_nodes[r, k] is a child of accepted_nodes[r, k - 1] in request r's tree; only the first accepted_count[r] entries are used. `accepted_count`: some request has exactly 8, some exactly 1.
All inputs are finite; a program needn't handle non-finite values.
Results may differ from a plain program's by a relative error of at most 0.0055.
Values may be sent and summed in bfloat16 or wider, within the bound.
No kernel may reach another device: no remote copies, remote signals or barrier semaphores. Data moves between devices by JAX's collectives and lax.ppermute only.
A program may use at most 64 MiB of HBM per device.

v0:
```python
import math
import jax
import jax.numpy as jnp
from jax import lax
from jax.sharding import PartitionSpec as P

HEAD_SIZE = 128
TREE_TOKENS = 64
ACC = 8
NEG_FLOOR = -1e30


def ancestors(parent_rows):
    node_ids = jnp.arange(TREE_TOKENS, dtype=jnp.int32)
    parent_link = (
        (parent_rows[:, :, None] == node_ids[None, None, :]) & (node_ids[None, :, None] >= 1)
    ).astype(jnp.float32)
    reachable = jnp.eye(TREE_TOKENS, dtype=jnp.float32)[None] + parent_link
    for doubling in range((TREE_TOKENS - 1).bit_length()):
        reachable = jnp.minimum(
            reachable
            + jnp.einsum("rij,rjk->rik", reachable, reachable, precision=lax.Precision.HIGHEST),
            1.0,
        )
    return reachable


def partial_softmax(query_vectors, key_rows, value_rows, usable, score_scale):
    scores = (
        jnp.einsum(
            "rtkgh,rbpkh->brkgtp", query_vectors, key_rows, preferred_element_type=jnp.float32
        )
        * score_scale
    )
    scores = jnp.where(usable, scores, NEG_FLOOR)
    peak_score = jnp.max(scores, axis=-1)
    weights = jnp.where(usable, jnp.exp(scores - peak_score[..., None]), 0.0)
    weight_sum = jnp.sum(weights, axis=-1)
    weighted = jnp.einsum(
        "brkgtp,rbpkh->brtkgh",
        weights.astype(jnp.bfloat16),
        value_rows,
        preferred_element_type=jnp.float32,
    )
    block_count, req_count, kv_count, query_group_width, row_count = peak_score.shape
    weighted = weighted.reshape(
        block_count, req_count * row_count, kv_count * query_group_width * value_rows.shape[-1]
    )
    peak_score = peak_score.transpose(0, 1, 4, 2, 3).reshape(
        block_count, req_count * row_count, kv_count * query_group_width
    )
    weight_sum = weight_sum.transpose(0, 1, 4, 2, 3).reshape(
        block_count, req_count * row_count, kv_count * query_group_width
    )
    return (weighted, peak_score, weight_sum)


def merge_parts(cache_part, draft_part, head_dim):
    cache_out, cache_peak, cache_sum = cache_part
    draft_out, draft_peak, draft_sum = draft_part
    cache_out = cache_out.astype(jnp.float32)
    overall = jnp.maximum(jnp.max(cache_peak, axis=0), draft_peak[0])
    cache_factor = jnp.exp(cache_peak - overall[None])
    draft_factor = jnp.exp(draft_peak[0] - overall)
    denominator = jnp.sum(cache_factor * cache_sum, axis=0) + draft_factor * draft_sum[0]
    block_count, row_count, head_count = cache_peak.shape
    numerator = jnp.sum(
        cache_factor[..., None] * cache_out.reshape(block_count, row_count, head_count, head_dim),
        axis=0,
    )
    numerator = numerator + draft_factor[..., None] * draft_out[0].reshape(
        row_count, head_count, head_dim
    )
    return (
        (numerator / denominator[..., None])
        .reshape(row_count, head_count * head_dim)
        .astype(jnp.bfloat16)
    )


def place_rows(sources, slot_index, written, cache_rows):
    slot_ids = jnp.arange(sources.shape[1], dtype=jnp.int32)
    selector = ((slot_index[:, :, None] == slot_ids[None, None, :]) & written[:, :, None]).astype(
        jnp.bfloat16
    )
    placed = jnp.einsum(
        "rps,rsc->rpc", selector, sources, preferred_element_type=jnp.float32
    ).astype(jnp.bfloat16)
    return jnp.where(written[:, :, None], placed, cache_rows)


def on_device(
    queries,
    draft_token_keys,
    draft_token_values,
    cached_key_vectors,
    cached_value_vectors,
    out_weight,
    lengths,
    parents,
    accepted_nodes,
    accepted_count,
):
    block_count = lax.axis_size("blk")
    my_block = lax.axis_index("blk")
    rows_dev, width_q = queries.shape
    requests = lengths.shape[0]
    cache_width = cached_key_vectors.shape[2]
    kv_local = cache_width // HEAD_SIZE
    query_group_width = width_q // (kv_local * HEAD_SIZE)
    block_len = cached_key_vectors.shape[1]
    score_scale = 1.0 / math.sqrt(HEAD_SIZE)
    leading_row = my_block * rows_dev
    my_request = leading_row // TREE_TOKENS
    node_start = leading_row - my_request * TREE_TOKENS
    local_queries = queries.reshape(1, rows_dev, kv_local, query_group_width, HEAD_SIZE)
    gathered_keys, gathered_values = (
        lax.all_gather(draft_token_keys, "blk", axis=0, tiled=True),
        lax.all_gather(draft_token_values, "blk", axis=0, tiled=True),
    )
    tree_keys = lax.dynamic_slice_in_dim(
        gathered_keys, my_request * TREE_TOKENS, TREE_TOKENS, 0
    ).reshape(1, 1, TREE_TOKENS, kv_local, HEAD_SIZE)
    tree_values = lax.dynamic_slice_in_dim(
        gathered_values, my_request * TREE_TOKENS, TREE_TOKENS, 0
    ).reshape(1, 1, TREE_TOKENS, kv_local, HEAD_SIZE)
    reachable = ancestors(lax.dynamic_slice_in_dim(parents, my_request, 1, 0))
    own_reach = lax.dynamic_slice_in_dim(reachable, node_start, rows_dev, 1)
    draft_usable = (own_reach > 0.5)[None, :, None, None, :, :]
    draft_part = partial_softmax(local_queries, tree_keys, tree_values, draft_usable, score_scale)
    every_query = lax.all_gather(queries, "blk", axis=0, tiled=True)
    all_queries = every_query.reshape(requests, TREE_TOKENS, kv_local, query_group_width, HEAD_SIZE)
    positions = my_block * block_len + jnp.arange(block_len, dtype=jnp.int32)
    usable = (positions[None, :] < lengths[:, None])[None, :, None, None, None, :]
    local_out, local_peak, local_sum = partial_softmax(
        all_queries,
        cached_key_vectors.reshape(requests, 1, block_len, kv_local, HEAD_SIZE),
        cached_value_vectors.reshape(requests, 1, block_len, kv_local, HEAD_SIZE),
        usable,
        score_scale,
    )
    moved_out = lax.all_to_all(
        local_out[0].astype(jnp.bfloat16), "blk", split_axis=0, concat_axis=0, tiled=True
    )
    moved_peak, moved_sum = (
        lax.all_to_all(local_peak[0], "blk", split_axis=0, concat_axis=0, tiled=True),
        lax.all_to_all(local_sum[0], "blk", split_axis=0, concat_axis=0, tiled=True),
    )
    cache_part = (
        moved_out.reshape(block_count, rows_dev, -1),
        moved_peak.reshape(block_count, rows_dev, -1),
        moved_sum.reshape(block_count, rows_dev, -1),
    )
    attention = merge_parts(cache_part, draft_part, HEAD_SIZE)
    every_row = lax.all_gather(attention, "blk", axis=0, tiled=True)
    projected = lax.psum_scatter(
        jnp.dot(every_row, out_weight, preferred_element_type=jnp.float32),
        "kv",
        scatter_dimension=0,
        tiled=True,
    ).astype(jnp.bfloat16)
    positions_here = my_block * block_len + jnp.arange(block_len, dtype=jnp.int32)
    offset = positions_here[None, :] - lengths[:, None]
    written = (offset >= 0) & (offset < accepted_count[:, None])
    slot_match = offset[:, :, None] == jnp.arange(ACC, dtype=jnp.int32)[None, None, :]
    node_ids = jnp.sum(jnp.where(slot_match, accepted_nodes[:, None, :], 0), axis=-1)
    new_cache_keys = place_rows(
        gathered_keys.reshape(requests, TREE_TOKENS, cache_width),
        node_ids,
        written,
        cached_key_vectors,
    )
    new_cache_values = place_rows(
        gathered_values.reshape(requests, TREE_TOKENS, cache_width),
        node_ids,
        written,
        cached_value_vectors,
    )
    return (projected, new_cache_keys, new_cache_values)


def solution(mesh):
    return jax.shard_map(
        on_device,
        mesh=mesh,
        in_specs=(
            P("blk", "kv"),
            P("blk", "kv"),
            P("blk", "kv"),
            P(None, "blk", "kv"),
            P(None, "blk", "kv"),
            P("kv", "blk"),
            P(),
            P(),
            P(),
            P(),
        ),
        out_specs=(P("kv", "blk"), P(None, "blk", "kv"), P(None, "blk", "kv")),
        check_vma=False,
    )
```

profile of v0, /device:TPU:4, one launch (start us, length us, event | category | flops | bytes accessed | tf_op | source)
XLA Modules:
  0.0 283.2 jit_solution(6626827668490179836)
XLA Ops:
  7.2 52.1 %all_gather.12 = bf16[256,1024]{1,0:T(8,128)(2,1)S(1)} all-gather(bf16[8,1024]{1,0:T(8,128)(2,1)} %param.10), channel_id=1, replica_groups=mesh['kv'=8,'blk'=32] {'blk'}, dimensions={0}, use_global_device_ids=true | all-gather | bytes 540672 | tf_op jit(solution)/shard_map/all_gather | solution.py:131
  59.5 0.5 copy-done.6
  60.3 0.5 fusion.53
  60.9 0.7 copy.63
  61.7 7.0 %all-to-all-start = ((f32[32,8,8]{1,2,0:T(8,128)}), f32[32,8,8]{1,2,0:T(8,128)S(1)}, u32[]{:S(2)}, u32[]{:S(2)}) async-start(f32[32,8,8]{1,2,0:T(8,128)} %copy.63), calls=%async_computation | async-start | bytes 262144 | tf_op jit(solution)/shard_map/all_to_all | solution.py:146
  68.7 0.7 fusion.51
  70.6 0.6 fusion.18
  71.5 0.5 fusion.3
  72.1 0.7 copy.73
  73.2 1.0 convert_element_type.101
  74.2 2.8 all-to-all-done
  77.0 7.1 %all-to-all-start.2 = ((f32[32,8,8]{1,2,0:T(8,128)}), f32[32,8,8]{1,2,0:T(8,128)S(1)}, u32[]{:S(2)}, u32[]{:S(2)}) async-start(f32[32,8,8]{1,2,0:T(8,128)} %copy.73), calls=%async_computation.2 | async-start | bytes 262144 | tf_op jit(solution)/shard_map/all_to_all | solution.py:147
  84.2 49.3 %all_gather.13 = bf16[256,128]{1,0:T(8,128)(2,1)S(1)} all-gather(bf16[8,128]{1,0:T(8,128)(2,1)S(1)} %copy-done.3), channel_id=1, replica_groups=mesh['kv'=8,'blk'=32] {'blk'}, dimensions={0}, use_global_device_ids=true | all-gather | bytes 67584 | tf_op jit(solution)/shard_map/all_gather | solution.py:118
  133.5 7.9 %all-to-all-start.1 = ((bf16[32,8,1024]{2,1,0:T(8,128)(2,1)}), bf16[32,8,1024]{2,1,0:T(8,128)(2,1)S(1)}, u32[]{:S(2)}, u32[]{:S(2)}) async-start(bf16[32,8,1024]{2,1,0:T(8,128)(2,1)} %convert_element_type.101), calls=%async_computation.1 | async-start | bytes 1048576 | tf_op jit(solution)/shard_map/all_to_all | solution.py:142
  141.9 0.6 copy-done.4
  142.6 49.7 %all_gather.14 = bf16[256,128]{1,0:T(8,128)(2,1)S(1)} all-gather(bf16[8,128]{1,0:T(8,128)(2,1)S(1)} %copy-done.4), channel_id=1, replica_groups=mesh['kv'=8,'blk'=32] {'blk'}, dimensions={0}, use_global_device_ids=true | all-gather | bytes 67584 | tf_op jit(solution)/shard_map/all_gather | solution.py:119
  192.4 0.3 fusion.17
  192.9 47.4 %all_gather.15 = bf16[256,1024]{1,0:T(8,128)(2,1)S(1)} all-gather(bf16[8,1024]{1,0:T(8,128)(2,1)S(1)} %fusion.15), channel_id=1, replica_groups=mesh['kv'=8,'blk'=32] {'blk'}, dimensions={0}, use_global_device_ids=true | all-gather | bytes 540672 | tf_op jit(solution)/shard_map/all_gather | solution.py:155
  240.3 1.0 fusion.56
  241.3 0.7 copy-done.5
  242.0 0.9 fusion.4
  243.0 0.9 fusion.5
  243.9 31.1 %reduce-scatter.2.cloned.1.call-done = f32[32,256]{1,0:T(8,128)} async-done(((f32[256,256]{1,0:T(8,128)}), f32[32,256]{1,0:T(8,128)}) %reduce-scatter.2.cloned.1.call-update) | async-done | bytes 32784 | tf_op jit(solution)/shard_map/reduce_scatter | solution.py:156
  274.9 1.4 convert_element_type.105
  (47 shorter events, 3.4 us)
Async XLA Ops:
  7.2 233.1 %copy-start = (bf16[1024,256]{1,0:T(8,128)(2,1)S(1)}, bf16[1024,256]{1,0:T(8,128)(2,1)}, u32[]{:S(2)}) copy-start(bf16[1024,256]{1,0:T(8,128)(2,1)} %param.15) | copy-start | bytes 1572868
  59.3 0.7 copy-start.6
  59.3 0.7 copy-start.7
  59.3 0.9 copy-start.8
  61.7 15.4 %all-to-all-start = ((f32[32,8,8]{1,2,0:T(8,128)}), f32[32,8,8]{1,2,0:T(8,128)S(1)}, u32[]{:S(2)}, u32[]{:S(2)}) async-start(f32[32,8,8]{1,2,0:T(8,128)} %copy.63), calls=%async_computation | async-start | bytes 262144 | tf_op jit(solution)/shard_map/all_to_all | solution.py:146
  70.6 0.9 copy-start.1
  74.2 9.9 %copy-start.3 = (bf16[8,128]{1,0:T(8,128)(2,1)S(1)}, bf16[8,128]{1,0:T(8,128)(2,1)}, u32[]{:S(2)}) copy-start(bf16[8,128]{1,0:T(8,128)(2,1)} %param.11) | copy-start | bytes 6148
  77.0 56.4 %all-to-all-start.2 = ((f32[32,8,8]{1,2,0:T(8,128)}), f32[32,8,8]{1,2,0:T(8,128)S(1)}, u32[]{:S(2)}, u32[]{:S(2)}) async-start(f32[32,8,8]{1,2,0:T(8,128)} %copy.73), calls=%async_computation.2 | async-start | bytes 262144 | tf_op jit(solution)/shard_map/all_to_all | solution.py:147
  133.4 8.0 %copy-start.2 = (bf16[8,1024]{1,0:T(8,128)(2,1)S(1)}, bf16[8,1024]{1,0:T(8,128)(2,1)}, u32[]{:S(2)}) copy-start(bf16[8,1024]{1,0:T(8,128)(2,1)} %param.10) | copy-start | bytes 49156
  133.5 59.0 %all-to-all-start.1 = ((bf16[32,8,1024]{2,1,0:T(8,128)(2,1)}), bf16[32,8,1024]{2,1,0:T(8,128)(2,1)S(1)}, u32[]{:S(2)}, u32[]{:S(2)}) async-start(bf16[32,8,1024]{2,1,0:T(8,128)(2,1)} %convert_element_type.101), calls=%async_computation.1 | async-start | bytes 1048576 | tf_op jit(solution)/shard_map/all_to_all | solution.py:142
  141.4 133.6 %reduce-scatter.2.cloned.1.call-start = ((), (), s32[]{:S(2)}) async-start(), calls=%async_computation.4 | async-start | bytes 294912 | tf_op jit(solution)/shard_map/reduce_scatter | solution.py:156
  141.9 0.7 copy-start.4
  241.3 0.7 copy-start.5
Sparse Core Ops, SparseCore 0:
  241.4 33.4 reduce-scatter.1
where the time goes:
time: 284 us; the launch traced here: 283 us
  blocking collectives  198 us (70%)
  waiting for transfers between devices  33.9 us (12%)
  starting transfers between devices  22 us (8%)
  between operations  14.3 us (5%)
  local copies, waits for them, and re-layouts  6.25 us (2%)
  matrix products  5.14 us (2%)
  other arithmetic  3.09 us (1%)
    all_gather x1, blocking collectives, on_device(): every_query = lax.all_gather(queries, 'blk', axis=0, tiled=True)  52.1 us
    all_gather x1, blocking collectives, on_device(): lax.all_gather(draft_token_values, 'blk', axis=0, tiled=True)  49.7 us
    all_gather x1, blocking collectives, on_device(): lax.all_gather(draft_token_keys, 'blk', axis=0, tiled=True)  49.3 us
    all_gather x1, blocking collectives, on_device(): every_row = lax.all_gather(attention, 'blk', axis=0, tiled=True)  47.4 us
    reduce_scatter x1, waiting for transfers between devices, on_device(): lax.psum_scatter(jnp.dot(every_row, out_weight, preferred_element_type=jn...  31.1 us
    all_to_all x1, starting transfers between devices, on_device(): lax.all_to_all(local_out[0].astype(jnp.bfloat16), 'blk', split_axis=0, co...  7.89 us
    all_to_all x1, starting transfers between devices, on_device(): lax.all_to_all(local_sum[0], 'blk', split_axis=0, concat_axis=0, tiled=True)  7.09 us
    all_to_all x1, starting transfers between devices, on_device(): lax.all_to_all(local_peak[0], 'blk', split_axis=0, concat_axis=0, tiled=T...  6.95 us
  transfers between devices with their start and end apart: 4, of which 2 were waited for; matrix products, arithmetic and copies ran while one was open for 3% of the time, Pallas kernels for 0%

commit v1 on v0

--- a/solution.py
+++ b/solution.py
@@ -116,7 +116,15 @@
     local_queries = queries.reshape(1, rows_dev, kv_local, query_group_width, HEAD_SIZE)
     gathered_keys, gathered_values = (
         lax.all_gather(draft_token_keys, "blk", axis=0, tiled=True),
-        lax.all_gather(draft_token_values, "blk", axis=0, tiled=True),
+        jnp.concatenate(
+            lax.all_to_all(
+                jnp.stack([draft_token_values] * lax.axis_size("blk"), 0),
+                axis_name="blk",
+                split_axis=0,
+                concat_axis=0,
+            ),
+            0,
+        ),
     )
     tree_keys = lax.dynamic_slice_in_dim(
         gathered_keys, my_request * TREE_TOKENS, TREE_TOKENS, 0

time: 284 us -> 258 us (0.908)
  blocking collectives: 198 us -> 149 us
  waiting for transfers between devices: 33.9 us -> 50 us
  starting transfers between devices: 22 us -> 29.5 us
    all_gather x1 -> x0, blocking collectives: 49.7 us -> none  [on_device(): lax.all_gather(draft_token_values, 'blk', axis=0, tiled=True)]
    all_to_all x1, waiting for transfers between devices: 0.01 us -> 10.1 us  [on_device(): lax.all_to_all(local_out[0].astype(jnp.bfloat16), 'blk', split_axis=0, co...]
    all_to_all x0 -> x1, waiting for transfers between devices: none -> 7.62 us  [on_device(): lax.all_to_all(jnp.stack([draft_token_values] * lax.axis_size('blk'), 0),...]
    all_to_all x0 -> x1, starting transfers between devices: none -> 7.5 us  [on_device(): lax.all_to_all(jnp.stack([draft_token_values] * lax.axis_size('blk'), 0),...]
  transfers between devices with their start and end apart: 4 -> 5, of which waited for: 2 -> 4; matrix products, arithmetic and copies ran while one was open for 3% -> 3% of each run, Pallas kernels for 0% -> 0%
where the time goes in v1:
time: 258 us; the launch traced here: 257 us
  blocking collectives  149 us (58%)
  waiting for transfers between devices  50 us (19%)
  starting transfers between devices  29.5 us (11%)
  between operations  14.3 us (6%)
  local copies, waits for them, and re-layouts  6.28 us (2%)
  matrix products  5.14 us (2%)
  other arithmetic  3.08 us (1%)
    all_gather x1, blocking collectives, on_device(): every_query = lax.all_gather(queries, 'blk', axis=0, tiled=True)  52.1 us
    all_gather x1, blocking collectives, on_device(): lax.all_gather(draft_token_keys, 'blk', axis=0, tiled=True)  49.3 us
    all_gather x1, blocking collectives, on_device(): every_row = lax.all_gather(attention, 'blk', axis=0, tiled=True)  47.6 us
    reduce_scatter x1, waiting for transfers between devices, on_device(): lax.psum_scatter(jnp.dot(every_row, out_weight, preferred_element_type=jn...  29.5 us
    all_to_all x1, waiting for transfers between devices, on_device(): lax.all_to_all(local_out[0].astype(jnp.bfloat16), 'blk', split_axis=0, co...  10.1 us
    all_to_all x1, starting transfers between devices, on_device(): lax.all_to_all(local_out[0].astype(jnp.bfloat16), 'blk', split_axis=0, co...  7.89 us
    all_to_all x1, waiting for transfers between devices, on_device(): lax.all_to_all(jnp.stack([draft_token_values] * lax.axis_size('blk'), 0),...  7.62 us
    all_to_all x1, starting transfers between devices, on_device(): lax.all_to_all(jnp.stack([draft_token_values] * lax.axis_size('blk'), 0),...  7.5 us
  transfers between devices with their start and end apart: 5, of which 4 were waited for; matrix products, arithmetic and copies ran while one was open for 3% of the time, Pallas kernels for 0%

profile of v1, /device:TPU:4, one launch (start us, length us, event | category | flops | bytes accessed | tf_op | source)
XLA Modules:
  0.0 257.3 jit_solution(16718428132875171701)
XLA Ops:
  7.2 52.1 %all_gather.9 = bf16[256,1024]{1,0:T(8,128)(2,1)S(1)} all-gather(bf16[8,1024]{1,0:T(8,128)(2,1)} %param.10), channel_id=1, replica_groups=mesh['kv'=8,'blk'=32] {'blk'}, dimensions={0}, use_global_device_ids=true | all-gather | bytes 540672 | tf_op jit(solution)/shard_map/all_gather | solution.py:139
  59.5 0.5 copy-done.6
  60.3 0.5 fusion.53
  60.9 0.7 copy.63
  61.7 7.0 %all-to-all-start = ((f32[32,8,8]{1,2,0:T(8,128)}), f32[32,8,8]{1,2,0:T(8,128)S(1)}, u32[]{:S(2)}, u32[]{:S(2)}) async-start(f32[32,8,8]{1,2,0:T(8,128)} %copy.63), calls=%async_computation | async-start | bytes 262144 | tf_op jit(solution)/shard_map/all_to_all | solution.py:154
  68.7 0.7 fusion.51
  70.6 0.6 fusion.18
  72.1 0.7 copy.73
  73.2 1.0 convert_element_type.101
  74.2 2.8 %all-to-all-done = f32[32,8,8]{1,2,0:T(8,128)S(1)} async-done(((f32[32,8,8]{1,2,0:T(8,128)}), f32[32,8,8]{1,2,0:T(8,128)S(1)}, u32[]{:S(2)}, u32[]{:S(2)}) %all-to-all-start) | async-done | bytes 8224 | tf_op jit(solution)/shard_map/all_to_all | solution.py:154
  77.0 7.1 %all-to-all-start.3 = ((f32[32,8,8]{1,2,0:T(8,128)}), f32[32,8,8]{1,2,0:T(8,128)S(1)}, u32[]{:S(2)}, u32[]{:S(2)}) async-start(f32[32,8,8]{1,2,0:T(8,128)} %copy.73), calls=%async_computation.3 | async-start | bytes 262144 | tf_op jit(solution)/shard_map/all_to_all | solution.py:155
  84.2 49.3 %all_gather.10 = bf16[256,128]{1,0:T(8,128)(2,1)S(1)} all-gather(bf16[8,128]{1,0:T(8,128)(2,1)S(1)} %copy-done.3), channel_id=1, replica_groups=mesh['kv'=8,'blk'=32] {'blk'}, dimensions={0}, use_global_device_ids=true | all-gather | bytes 67584 | tf_op jit(solution)/shard_map/all_gather | solution.py:118
  133.5 7.9 %all-to-all-start.1 = ((bf16[32,8,1024]{2,1,0:T(8,128)(2,1)}), bf16[32,8,1024]{2,1,0:T(8,128)(2,1)S(1)}, u32[]{:S(2)}, u32[]{:S(2)}) async-start(bf16[32,8,1024]{2,1,0:T(8,128)(2,1)} %convert_element_type.101), calls=%async_computation.1 | async-start | bytes 1048576 | tf_op jit(solution)/shard_map/all_to_all | solution.py:150
  142.1 10.1 %all-to-all-done.1 = bf16[32,8,1024]{2,1,0:T(8,128)(2,1)S(1)} async-done(((bf16[32,8,1024]{2,1,0:T(8,128)(2,1)}), bf16[32,8,1024]{2,1,0:T(8,128)(2,1)S(1)}, u32[]{:S(2)}, u32[]{:S(2)}) %all-to-all-start.1) | async-done | bytes 524320 | tf_op jit(solution)/shard_map/all_to_all | solution.py:150
  152.2 0.6 stack.2
  152.8 7.5 %all-to-all-start.2 = ((bf16[32,8,128]{2,1,0:T(8,128)(2,1)}), bf16[32,8,128]{2,1,0:T(8,128)(2,1)S(1)}, u32[]{:S(2)}, u32[]{:S(2)}) async-start(bf16[32,8,128]{2,1,0:T(8,128)(2,1)} %stack.2), calls=%async_computation.2 | async-start | bytes 131072 | tf_op jit(solution)/shard_map/all_to_all | solution.py:120
  160.7 7.6 %all-to-all-done.2 = bf16[32,8,128]{2,1,0:T(8,128)(2,1)S(1)} async-done(((bf16[32,8,128]{2,1,0:T(8,128)(2,1)}), bf16[32,8,128]{2,1,0:T(8,128)(2,1)S(1)}, u32[]{:S(2)}, u32[]{:S(2)}) %all-to-all-start.2) | async-done | bytes 65568 | tf_op jit(solution)/shard_map/all_to_all | solution.py:120
  168.5 47.6 %all_gather.11 = bf16[256,1024]{1,0:T(8,128)(2,1)S(1)} all-gather(bf16[8,1024]{1,0:T(8,128)(2,1)S(1)} %fusion.15), channel_id=1, replica_groups=mesh['kv'=8,'blk'=32] {'blk'}, dimensions={0}, use_global_device_ids=true | all-gather | bytes 540672 | tf_op jit(solution)/shard_map/all_gather | solution.py:163
  216.0 1.0 fusion.56
  217.0 0.7 copy-done.5
  217.8 0.9 fusion.4
  218.7 0.9 fusion.5
  219.6 29.5 %reduce-scatter.2.cloned.1.call-done = f32[32,256]{1,0:T(8,128)} async-done(((f32[256,256]{1,0:T(8,128)}), f32[32,256]{1,0:T(8,128)}) %reduce-scatter.2.cloned.1.call-update) | async-done | bytes 32784 | tf_op jit(solution)/shard_map/reduce_scatter | solution.py:164
  249.1 1.4 convert_element_type.105
  (49 shorter events, 4.2 us)
Async XLA Ops:
  7.2 208.9 %copy-start = (bf16[1024,256]{1,0:T(8,128)(2,1)S(1)}, bf16[1024,256]{1,0:T(8,128)(2,1)}, u32[]{:S(2)}) copy-start(bf16[1024,256]{1,0:T(8,128)(2,1)} %param.15) | copy-start | bytes 1572868
  59.3 0.7 copy-start.6
  59.3 0.7 copy-start.7
  59.3 0.9 copy-start.8
  61.7 15.4 %all-to-all-start = ((f32[32,8,8]{1,2,0:T(8,128)}), f32[32,8,8]{1,2,0:T(8,128)S(1)}, u32[]{:S(2)}, u32[]{:S(2)}) async-start(f32[32,8,8]{1,2,0:T(8,128)} %copy.63), calls=%async_computation | async-start | bytes 262144 | tf_op jit(solution)/shard_map/all_to_all | solution.py:154
  70.6 0.9 copy-start.1
  74.2 9.9 %copy-start.3 = (bf16[8,128]{1,0:T(8,128)(2,1)S(1)}, bf16[8,128]{1,0:T(8,128)(2,1)}, u32[]{:S(2)}) copy-start(bf16[8,128]{1,0:T(8,128)(2,1)} %param.11) | copy-start | bytes 6148
  77.0 56.4 %all-to-all-start.3 = ((f32[32,8,8]{1,2,0:T(8,128)}), f32[32,8,8]{1,2,0:T(8,128)S(1)}, u32[]{:S(2)}, u32[]{:S(2)}) async-start(f32[32,8,8]{1,2,0:T(8,128)} %copy.73), calls=%async_computation.3 | async-start | bytes 262144 | tf_op jit(solution)/shard_map/all_to_all | solution.py:155
  133.4 7.9 %copy-start.2 = (bf16[8,1024]{1,0:T(8,128)(2,1)S(1)}, bf16[8,1024]{1,0:T(8,128)(2,1)}, u32[]{:S(2)}) copy-start(bf16[8,1024]{1,0:T(8,128)(2,1)} %param.10) | copy-start | bytes 49156
  133.5 18.7 %all-to-all-start.1 = ((bf16[32,8,1024]{2,1,0:T(8,128)(2,1)}), bf16[32,8,1024]{2,1,0:T(8,128)(2,1)S(1)}, u32[]{:S(2)}, u32[]{:S(2)}) async-start(bf16[32,8,1024]{2,1,0:T(8,128)(2,1)} %convert_element_type.101), calls=%async_computation.1 | async-start | bytes 1048576 | tf_op jit(solution)/shard_map/all_to_all | solution.py:150
  142.1 10.1 %copy-start.4 = (bf16[8,128]{1,0:T(8,128)(2,1)S(1)}, bf16[8,128]{1,0:T(8,128)(2,1)}, u32[]{:S(2)}) copy-start(bf16[8,128]{1,0:T(8,128)(2,1)} %param.12) | copy-start | bytes 6148
  152.8 15.5 %all-to-all-start.2 = ((bf16[32,8,128]{2,1,0:T(8,128)(2,1)}), bf16[32,8,128]{2,1,0:T(8,128)(2,1)S(1)}, u32[]{:S(2)}, u32[]{:S(2)}) async-start(bf16[32,8,128]{2,1,0:T(8,128)(2,1)} %stack.2), calls=%async_computation.2 | async-start | bytes 131072 | tf_op jit(solution)/shard_map/all_to_all | solution.py:120
  160.3 88.7 %reduce-scatter.2.cloned.1.call-start = ((), (), s32[]{:S(2)}) async-start(), calls=%async_computation.5 | async-start | bytes 294912 | tf_op jit(solution)/shard_map/reduce_scatter | solution.py:164
  217.0 0.7 copy-start.5
Sparse Core Ops, SparseCore 0:
  217.2 31.8 reduce-scatter.1
